TPU v7x, 32 devices: a whole 2x2x4 slice. The times are simulated.
32 devices in a mesh: grp: 2 (over y), cell: 8 (over z, x), gene: 2 (over core).
Axes of the slice: x: 2, y: 2, z: 4, core: 2. Of those that a mesh axis runs over, the one named last changes fastest.
Arguments:
- expression: bfloat16 [2048, 16384], P(('grp', 'cell'), 'gene'), parts along dimension 0, may hold values from -6 to 6
- design: bfloat16 [2048, 128], P(('grp', 'cell')), parts along dimension 0, may hold values from -24 to 24
- quantile_level: float32 [16384], P('gene'), may hold values from 0.1 to 0.9
Outputs:
- quantile_slack: bfloat16 [2048, 16384], P(('grp', 'cell'), 'gene'), parts along dimension 0
- low_rank_coef: float32 [32768, 128], P(('grp', 'gene', 'cell')), parts along dimension 0
There are 2 independent parts, one for each index of `grp`. A program takes and returns all parts, laid end to end along the dimension named above; an argument that names none is the same for every part. Nothing has to cross between parts.
All inputs are finite; a program needn't handle non-finite values.
Results may differ from a plain program's by a relative error of at most 0.0025.
The roundings to bfloat16 on the way count: a program that leaves them out, or rounds other values in their place, can miss the bound.
Values may be sent and summed in bfloat16 or wider, within the bound.
No kernel may reach another device: no remote copies, remote signals or barrier semaphores. Data moves between devices by JAX's collectives and lax.ppermute only.
A program may use at most 64 MiB of HBM per device.

v0:
```python
import functools
import math
import jax
import jax.numpy as jnp
from jax import lax
from jax.sharding import PartitionSpec as P

NS_STEPS = 8
shrink_rate = 0.25


def matmul(left, right):
    return jnp.dot(left, right, precision=lax.Precision.HIGHEST)


def invert(matrix):
    identity = jnp.eye(matrix.shape[0], dtype=jnp.float32)
    factor = jnp.linalg.cholesky(matrix)
    lower_inv = lax.linalg.triangular_solve(factor, identity, left_side=True, lower=True)
    return matmul(lower_inv.T, lower_inv)


def newton(moment):
    identity = jnp.eye(moment.shape[0], dtype=jnp.float32)
    current = moment / jnp.trace(moment)
    root_inv = identity
    for sweep in range(NS_STEPS):
        middle = 1.5 * identity - 0.5 * matmul(root_inv, current)
        current = matmul(current, middle)
        root_inv = matmul(middle, root_inv)
    return root_inv


def cell_ring(mesh):
    devices = mesh.devices
    names = list(mesh.axis_names)
    index = [0] * len(names)
    index[names.index("cell")] = slice(None)
    line = list(devices[tuple(index)].reshape(-1))
    n = len(line)
    try:
        coords = [tuple(d.coords) for d in line]
    except (AttributeError, TypeError):
        return list(range(n))
    varying = [a for a in range(len(coords[0])) if len({c[a] for c in coords}) > 1]
    where = {c: i for i, c in enumerate(coords)}
    if len(varying) == 1:
        return sorted(range(n), key=lambda i: coords[i][varying[0]])
    if len(varying) != 2:
        return list(range(n))
    sizes = [len({c[a] for c in coords}) for a in varying]
    if sizes[0] * sizes[1] != n:
        return list(range(n))
    if sizes[0] % 2:
        varying, sizes = (varying[::-1], sizes[::-1])
        if sizes[0] % 2:
            return list(range(n))
    lows = [min((c[a] for c in coords)) for a in varying]
    path = []
    for u in range(sizes[0]):
        span = range(1, sizes[1]) if u % 2 == 0 else range(sizes[1] - 1, 0, -1)
        path += [(u, v) for v in span]
    path += [(u, 0) for u in range(sizes[0] - 1, -1, -1)]
    order = []
    for u, v in path:
        key = list(coords[0])
        key[varying[0]] = lows[0] + u
        key[varying[1]] = lows[1] + v
        order.append(where[tuple(key)])
    return order


def gather_blocks(block, axis):
    n = lax.axis_size(axis)
    me = lax.axis_index(axis)
    received = [block]
    for shift in range(1, n):
        pairs = [(i, (i + shift) % n) for i in range(n)]
        received.append(lax.ppermute(block, axis, pairs))
    stacked = jnp.stack(received)
    return jnp.take(stacked, (me - jnp.arange(n)) % n, axis=0)


def butterfly_sum(value, axis):
    n = lax.axis_size(axis)
    if n & n - 1:
        return lax.psum(value, axis)
    bit = 1
    while bit < n:
        pairs = [(i, i ^ bit) for i in range(n)]
        value = value + lax.ppermute(value, axis, pairs)
        bit *= 2
    return value


def per_device(ring, expression, design, quantile_level):
    n = len(ring)
    width = design.shape[1]
    span = expression.shape[1] // n
    identity = jnp.eye(width, dtype=jnp.float32)
    design_all = gather_blocks(design, "cell").reshape(-1, width)
    sent = expression + (design_all[0, 0] * 0).astype(expression.dtype)
    expression_genes = lax.all_to_all(sent, "cell", 1, 0, tiled=True)
    gram_total = lax.dot_general(
        design_all, design_all, (((0,), (0,)), ((), ())), preferred_element_type=jnp.float32
    )
    inverse = invert(gram_total + identity)
    crossed = lax.dot_general(
        expression_genes, design_all, (((0,), (0,)), ((), ())), preferred_element_type=jnp.float32
    )
    coef = matmul(crossed, inverse)
    local_moment = lax.dot_general(
        coef, coef, (((0,), (0,)), ((), ())), precision=lax.Precision.HIGHEST
    )
    chip_moment = butterfly_sum(local_moment, "gene")
    moment = jnp.sum(gather_blocks(chip_moment, "cell"), axis=0)
    root_inv = newton(moment)
    low_rank_coef = coef - shrink_rate / math.sqrt(width) * matmul(coef, root_inv)
    coef_low_t = coef.astype(jnp.bfloat16).T
    ring_arr = jnp.array(ring, dtype=jnp.int32)
    pos_arr = jnp.array([ring.index(i) for i in range(n)], dtype=jnp.int32)
    me = lax.axis_index("cell")
    pos = pos_arr[me]
    forward = [(ring[q], ring[(q + 1) % n]) for q in range(n)]
    backward = [(ring[(q + 1) % n], ring[q]) for q in range(n)]
    out = jnp.zeros(expression.shape, jnp.bfloat16)

    def place(out, block, owner):
        start = owner * span
        fitted = jnp.dot(design, block, preferred_element_type=jnp.float32)
        local = lax.dynamic_slice_in_dim(expression, start, span, axis=1).astype(jnp.float32)
        level = lax.dynamic_slice_in_dim(quantile_level, start, span)[None, :]
        slack = local - fitted
        piece = (slack - jnp.clip(slack, level - 1.0, level)).astype(jnp.bfloat16)
        return lax.dynamic_update_slice_in_dim(out, piece, start, axis=1)

    out = place(out, coef_low_t, me)
    ahead, behind = (coef_low_t, coef_low_t)
    for step in range(1, n // 2 + 1):
        ahead = lax.ppermute(ahead, "cell", forward)
        out = place(out, ahead, ring_arr[(pos - step) % n])
        if step <= (n - 1) // 2:
            behind = lax.ppermute(behind, "cell", backward)
            out = place(out, behind, ring_arr[(pos + step) % n])
    return (out, low_rank_coef)


def solution(mesh):
    placed = (P(("grp", "cell"), "gene"), P(("grp", "cell"), None), P("gene"))
    ring = cell_ring(mesh)
    return jax.shard_map(
        functools.partial(per_device, ring),
        mesh=mesh,
        in_specs=placed,
        out_specs=(P(("grp", "cell"), "gene"), P(("grp", "gene", "cell"), None)),
        check_vma=False,
    )
```

profile of v0, /device:TPU:0, one launch (start us, length us, event | category | flops | bytes accessed | tf_op | source)
XLA Modules:
  0.0 163.7 jit_solution(11076976861056799472)
XLA Ops:
  0.6 6.1 %collective-permute-start.6 = (bf16[128,128]{1,0:T(8,128)(2,1)}, bf16[128,128]{1,0:T(8,128)(2,1)S(1)}, u32[]{:S(2)}, u32[]{:S(2)}) collective-permute-start(bf16[128,128]{1,0:T(8,128)(2,1)} %param.6), channel_id=1, source_target_pairs={{0,14},{2,0},{4,2},{6,4},{8,6},{10,8},{12,10},{14,12},{1,15},{3,1}... | collective-permute-start | bytes 98312 | tf_op jit(solution)/shard_map/ppermute | solution.py:79
  7.1 3.0 %collective-permute-start.3 = (bf16[128,128]{1,0:T(8,128)(2,1)}, bf16[128,128]{1,0:T(8,128)(2,1)S(1)}, u32[]{:S(2)}, u32[]{:S(2)}) collective-permute-start(bf16[128,128]{1,0:T(8,128)(2,1)} %param.6), channel_id=1, source_target_pairs={{0,8},{2,10},{4,12},{6,14},{8,0},{10,2},{12,4},{14,6},{1,9},{3,11}... | collective-permute-start | bytes 98312 | tf_op jit(solution)/shard_map/ppermute | solution.py:79
  10.1 1.5 collective-permute-start
  11.7 0.8 constant_dynamic-update-slice_fusion.7
  13.1 3.2 %copy.43 = bf16[128,8192]{0,1:T(8,128)(2,1)S(1)} copy(bf16[128,8192]{1,0:T(8,128)(2,1)} %param.5) | data formatting | bytes 4194304 | tf_op args[0]
  16.3 0.7 collective-permute-done
  17.0 5.7 %collective-permute-done.1 = bf16[128,128]{1,0:T(8,128)(2,1)S(1)} collective-permute-done((bf16[128,128]{1,0:T(8,128)(2,1)S(1)}, bf16[128,128]{1,0:T(8,128)(2,1)S(1)}, u32[]{:S(2)}, u32[]{:S(2)}) %collective-permute-start.1) | collective-permute-done | bytes 32800 | tf_op jit(solution)/shard_map/ppermute | solution.py:79
  22.7 5.7 %collective-permute-done.2 = bf16[128,128]{1,0:T(8,128)(2,1)S(1)} collective-permute-done((bf16[128,128]{1,0:T(8,128)(2,1)S(1)}, bf16[128,128]{1,0:T(8,128)(2,1)S(1)}, u32[]{:S(2)}, u32[]{:S(2)}) %collective-permute-start.2) | collective-permute-done | bytes 32800 | tf_op jit(solution)/shard_map/ppermute | solution.py:79
  30.9 1.5 broadcast_add_fusion
  32.4 3.9 %copy.45 = bf16[128,8,1024]{2,0,1:T(8,128)(2,1)} copy(bf16[128,8,1024]{0,2,1:T(8,128)(2,1)} %bitcast.190) | data formatting | bytes 4194304 | tf_op jit(solution)/shard_map/all_to_all | solution.py:103
  36.3 4.5 %all-to-all-start = ((bf16[128,8,1024]{2,0,1:T(8,128)(2,1)}), bf16[128,8,1024]{2,0,1:T(8,128)(2,1)}, u32[]{:S(2)}, u32[]{:S(2)}) async-start(bf16[128,8,1024]{2,0,1:T(8,128)(2,1)} %copy.45), calls=%async_computation | async-start | bytes 4194304 | tf_op jit(solution)/shard_map/all_to_all | solution.py:103
  46.1 0.7 fusion.35
  51.3 0.6 broadcast_add_fusion.1
  52.4 11.7 %cholesky.29 = f32[128,128]{1,0:T(8,128)S(1)} custom-call(f32[128,128]{1,0:T(8,128)S(1)} %fusion.27), custom_call_target="Cholesky" | custom-call | tf_op jit(solution)/shard_map/jit(cholesky)/cholesky | solution.py:18
  64.2 0.6 compare_reduce_fusion
  64.8 0.7 fusion.23
  65.5 9.8 %custom-call.6 = f32[1,128,128]{1,2,0:T(8,128)S(1)} custom-call(f32[1,128,128]{2,1,0:T(8,128)S(1)} %fusion.23), custom_call_target="InvertDiagBlocksLowerTriangular" | custom-call | tf_op jit(solution)/shard_map/triangular_solve | solution.py:19
  75.8 9.4 %all-to-all-done = bf16[128,8,1024]{2,0,1:T(8,128)(2,1)} async-done(((bf16[128,8,1024]{2,0,1:T(8,128)(2,1)}), bf16[128,8,1024]{2,0,1:T(8,128)(2,1)}, u32[]{:S(2)}, u32[]{:S(2)}) %all-to-all-start) | async-done | bytes 2097184 | tf_op jit(solution)/shard_map/all_to_all | solution.py:103
  85.2 3.9 %copy.46 = bf16[128,8,1024]{0,2,1:T(8,128)(2,1)} copy(bf16[128,8,1024]{2,0,1:T(8,128)(2,1)} %all-to-all-done) | data formatting | bytes 4194304 | tf_op jit(solution)/shard_map/all_to_all | solution.py:103
  89.1 2.4 %fusion.2 = f32[1024,128]{1,0:T(8,128)S(1)} fusion(bf16[128,8,1024]{0,2,1:T(8,128)(2,1)} %copy.46, bf16[8,128,128]{2,1,0:T(8,128)(2,1)S(1)} %gather_fusion, pred[8]{0:T(512)(128)(4,1)S(1)} %compare_and_fusion), kind=kOutput, calls=%fused_computation.4 | convolution fusion | flops 268566528 | bytes 2883592 | tf_op jit(solution)/shard_map/dot_general | solution.py:108
  92.1 1.0 fusion.38
  93.1 1.3 collective-permute-start.8
  94.4 0.8 collective-permute-start.7
  95.7 0.9 collective-permute-done.14
  96.6 1.5 bitcast_dynamic-update-slice_fusion.7
  98.1 1.3 collective-permute-start.15
  99.3 1.5 broadcast_in_dim.41
  100.9 0.7 constant_dynamic-update-slice_fusion.15
  101.6 1.4 collective-permute-start.20
  103.6 1.4 collective-permute-done.15
  105.6 0.6 bitcast_dynamic-update-slice_fusion.6
  106.2 4.9 %collective-permute-done.16 = f32[128,128]{1,0:T(8,128)S(1)} collective-permute-done((f32[128,128]{1,0:T(8,128)S(1)}, f32[128,128]{1,0:T(8,128)S(1)}, u32[]{:S(2)}, u32[]{:S(2)}) %collective-permute-start.16) | collective-permute-done | bytes 65568 | tf_op jit(solution)/shard_map/ppermute | solution.py:79
  111.1 0.7 collective-permute-start.17
  111.8 0.6 bitcast_dynamic-update-slice_fusion.5
  112.4 4.8 %collective-permute-done.17 = f32[128,128]{1,0:T(8,128)S(1)} collective-permute-done((f32[128,128]{1,0:T(8,128)S(1)}, f32[128,128]{1,0:T(8,128)S(1)}, u32[]{:S(2)}, u32[]{:S(2)}) %collective-permute-start.17) | collective-permute-done | bytes 65568 | tf_op jit(solution)/shard_map/ppermute | solution.py:79
  117.2 1.2 collective-permute-start.18
  118.4 0.6 bitcast_dynamic-update-slice_fusion.4
  119.0 3.5 %collective-permute-done.18 = f32[128,128]{1,0:T(8,128)S(1)} collective-permute-done((f32[128,128]{1,0:T(8,128)S(1)}, f32[128,128]{1,0:T(8,128)S(1)}, u32[]{:S(2)}, u32[]{:S(2)}) %collective-permute-start.18) | collective-permute-done | bytes 65568 | tf_op jit(solution)/shard_map/ppermute | solution.py:79
  123.2 0.6 bitcast_dynamic-update-slice_fusion.2
  123.9 0.6 bitcast_dynamic-update-slice_fusion.1
  124.5 2.3 %collective-permute-done.21 = f32[128,128]{1,0:T(8,128)S(1)} collective-permute-done((f32[128,128]{1,0:T(8,128)S(1)}, f32[128,128]{1,0:T(8,128)S(1)}, u32[]{:S(2)}, u32[]{:S(2)}) %collective-permute-start.21) | collective-permute-done | bytes 65568 | tf_op jit(solution)/shard_map/ppermute | solution.py:79
  126.8 0.6 bitcast_dynamic-update-slice_fusion
  127.5 1.6 gather_fusion.1
  129.1 0.8 select_reduce_fusion
  130.5 0.8 fusion.21
  131.3 0.8 fusion.29
  136.6 1.4 fusion.13
  138.4 1.3 subtract_convert_fusion.6
  139.7 1.3 subtract_convert_fusion.5
  141.3 1.8 %collective-permute-start.10 = (bf16[128,1024]{0,1:T(8,128)(2,1)}, bf16[128,1024]{0,1:T(8,128)(2,1)S(1)}, u32[]{:S(2)}, u32[]{:S(2)}) collective-permute-start(bf16[128,1024]{0,1:T(8,128)(2,1)} %collective-permute-done.8), channel_id=1, source_target_pairs={{8,4},{12,8},{14,12},{10,14},{6,10},{2,6},{0,2},{4,0},{9,5},{13,9}... | collective-permute-start | bytes 786440 | tf_op jit(solution)/shard_map/ppermute | solution.py:143
  143.2 0.7 constant_dynamic-update-slice_fusion.14
  143.9 0.7 constant_dynamic-update-slice_fusion.13
  144.6 2.3 %collective-permute-done.9 = bf16[128,1024]{0,1:T(8,128)(2,1)S(1)} collective-permute-done((bf16[128,1024]{0,1:T(8,128)(2,1)}, bf16[128,1024]{0,1:T(8,128)(2,1)S(1)}, u32[]{:S(2)}, u32[]{:S(2)}) %collective-permute-start.9) | collective-permute-done | bytes 262176 | tf_op jit(solution)/shard_map/ppermute | solution.py:140
  147.5 1.5 collective-permute-done.10
  149.0 0.7 copy-done.7
  150.4 1.9 %collective-permute-start.12 = (bf16[128,1024]{0,1:T(8,128)(2,1)}, bf16[128,1024]{0,1:T(8,128)(2,1)S(1)}, u32[]{:S(2)}, u32[]{:S(2)}) collective-permute-start(bf16[128,1024]{0,1:T(8,128)(2,1)} %copy-done.7), channel_id=1, source_target_pairs={{8,4},{12,8},{14,12},{10,14},{6,10},{2,6},{0,2},{4,0},{9,5},{13,9}... | collective-permute-start | bytes 786440 | tf_op jit(solution)/shard_map/ppermute | solution.py:143
  152.3 0.7 constant_dynamic-update-slice_fusion.12
  153.0 0.7 constant_dynamic-update-slice_fusion.11
  153.7 2.4 %collective-permute-done.11 = bf16[128,1024]{0,1:T(8,128)(2,1)S(1)} collective-permute-done((bf16[128,1024]{0,1:T(8,128)(2,1)S(1)}, bf16[128,1024]{0,1:T(8,128)(2,1)S(1)}, u32[]{:S(2)}, u32[]{:S(2)}) %collective-permute-start.11) | collective-permute-done | bytes 262176 | tf_op jit(solution)/shard_map/ppermute | solution.py:140
  156.5 0.7 collective-permute-done.12
  157.8 0.7 constant_dynamic-update-slice_fusion.10
  158.6 0.7 constant_dynamic-update-slice_fusion.9
  159.3 3.2 %collective-permute-done.13 = bf16[128,1024]{0,1:T(8,128)(2,1)S(1)} collective-permute-done((bf16[128,1024]{0,1:T(8,128)(2,1)S(1)}, bf16[128,1024]{0,1:T(8,128)(2,1)S(1)}, u32[]{:S(2)}, u32[]{:S(2)}) %collective-permute-start.13) | collective-permute-done | bytes 262176 | tf_op jit(solution)/shard_map/ppermute | solution.py:140
  163.0 0.7 constant_dynamic-update-slice_fusion.8
  (96 shorter events, 15.1 us)
Async XLA Ops:
  0.6 27.9 %collective-permute-start.6 = (bf16[128,128]{1,0:T(8,128)(2,1)}, bf16[128,128]{1,0:T(8,128)(2,1)S(1)}, u32[]{:S(2)}, u32[]{:S(2)}) collective-permute-start(bf16[128,128]{1,0:T(8,128)(2,1)} %param.6), channel_id=1, source_target_pairs={{0,14},{2,0},{4,2},{6,4},{8,6},{10,8},{12,10},{14,12},{1,15},{3,1}... | collective-permute-start | bytes 98312 | tf_op jit(solution)/shard_map/ppermute | solution.py:79
  6.7 21.8 %collective-permute-start.5 = (bf16[128,128]{1,0:T(8,128)(2,1)}, bf16[128,128]{1,0:T(8,128)(2,1)S(1)}, u32[]{:S(2)}, u32[]{:S(2)}) collective-permute-start(bf16[128,128]{1,0:T(8,128)(2,1)} %param.6), channel_id=1, source_target_pairs={{0,12},{2,14},{4,0},{6,2},{8,4},{10,6},{12,8},{14,10},{1,13},{3,15... | collective-permute-start | bytes 98312 | tf_op jit(solution)/shard_map/ppermute | solution.py:79
  7.1 21.3 %collective-permute-start.4 = (bf16[128,128]{1,0:T(8,128)(2,1)}, bf16[128,128]{1,0:T(8,128)(2,1)S(1)}, u32[]{:S(2)}, u32[]{:S(2)}) collective-permute-start(bf16[128,128]{1,0:T(8,128)(2,1)} %param.6), channel_id=1, source_target_pairs={{0,10},{2,12},{4,14},{6,0},{8,2},{10,4},{12,6},{14,8},{1,11},{3,13... | collective-permute-start | bytes 98312 | tf_op jit(solution)/shard_map/ppermute | solution.py:79
  7.1 21.3 %collective-permute-start.3 = (bf16[128,128]{1,0:T(8,128)(2,1)}, bf16[128,128]{1,0:T(8,128)(2,1)S(1)}, u32[]{:S(2)}, u32[]{:S(2)}) collective-permute-start(bf16[128,128]{1,0:T(8,128)(2,1)} %param.6), channel_id=1, source_target_pairs={{0,8},{2,10},{4,12},{6,14},{8,0},{10,2},{12,4},{14,6},{1,9},{3,11}... | collective-permute-start | bytes 98312 | tf_op jit(solution)/shard_map/ppermute | solution.py:79
  10.1 6.8 %collective-permute-start = (bf16[128,128]{1,0:T(8,128)(2,1)}, bf16[128,128]{1,0:T(8,128)(2,1)S(1)}, u32[]{:S(2)}, u32[]{:S(2)}) collective-permute-start(bf16[128,128]{1,0:T(8,128)(2,1)} %param.6), channel_id=1, source_target_pairs={{0,2},{2,4},{4,6},{6,8},{8,10},{10,12},{12,14},{14,0},{1,3},{3,5},... | collective-permute-start | bytes 98312 | tf_op jit(solution)/shard_map/ppermute | solution.py:79
  11.7 77.5 %copy-start.6 = (pred[8]{0:T(512)(128)(4,1)}, pred[8]{0:T(512)(128)(4,1)S(1)}, u32[]{:S(2)}) copy-start(pred[8]{0:T(512)(128)(4,1)S(1)} %compare_and_fusion) | copy-start | bytes 28
  13.1 3.9 %copy-start = (bf16[128,128]{1,0:T(8,128)(2,1)S(1)}, bf16[128,128]{1,0:T(8,128)(2,1)}, u32[]{:S(2)}) copy-start(bf16[128,128]{1,0:T(8,128)(2,1)} %param.6) | copy-start | bytes 98308
  17.0 5.7 %collective-permute-start.1 = (bf16[128,128]{1,0:T(8,128)(2,1)S(1)}, bf16[128,128]{1,0:T(8,128)(2,1)S(1)}, u32[]{:S(2)}, u32[]{:S(2)}) collective-permute-start(bf16[128,128]{1,0:T(8,128)(2,1)S(1)} %copy-done), channel_id=1, source_target_pairs={{0,4},{2,6},{4,8},{6,10},{8,12},{10,14},{12,0},{14,2},{1,5},{3,7},... | collective-permute-start | bytes 98312 | tf_op jit(solution)/shard_map/ppermute | solution.py:79
  22.7 5.7 %collective-permute-start.2 = (bf16[128,128]{1,0:T(8,128)(2,1)S(1)}, bf16[128,128]{1,0:T(8,128)(2,1)S(1)}, u32[]{:S(2)}, u32[]{:S(2)}) collective-permute-start(bf16[128,128]{1,0:T(8,128)(2,1)S(1)} %copy-done), channel_id=1, source_target_pairs={{0,6},{2,8},{4,10},{6,12},{8,14},{10,0},{12,2},{14,4},{1,7},{3,9},... | collective-permute-start | bytes 98312 | tf_op jit(solution)/shard_map/ppermute | solution.py:79
  36.3 4.5 %copy-start.8 = (s32[8]{0:T(128)S(1)}, s32[8]{0:T(128)}, u32[]{:S(2)}) copy-start(s32[8]{0:T(128)} %constant.188.clone) | copy-start | bytes 100
  36.3 9.8 %copy-start.2 = (s32[8]{0:T(128)S(1)}, s32[8]{0:T(128)}, u32[]{:S(2)}) copy-start(s32[8]{0:T(128)} %constant.187.clone) | copy-start | bytes 100
  36.3 15.0 %copy-start.1 = (f32[8192]{0:T(1024)S(1)}, f32[8192]{0:T(1024)}, u32[]{:S(2)}) copy-start(f32[8192]{0:T(1024)} %param.7) | copy-start | bytes 98308
  36.3 48.9 %all-to-all-start = ((bf16[128,8,1024]{2,0,1:T(8,128)(2,1)}), bf16[128,8,1024]{2,0,1:T(8,128)(2,1)}, u32[]{:S(2)}, u32[]{:S(2)}) async-start(bf16[128,8,1024]{2,0,1:T(8,128)(2,1)} %copy.45), calls=%async_computation | async-start | bytes 4194304 | tf_op jit(solution)/shard_map/all_to_all | solution.py:103
  93.1 46.6 %collective-permute-start.8 = (bf16[128,1024]{0,1:T(8,128)(2,1)S(1)}, bf16[128,1024]{0,1:T(8,128)(2,1)}, u32[]{:S(2)}, u32[]{:S(2)}) collective-permute-start(bf16[128,1024]{0,1:T(8,128)(2,1)S(1)} %convert_bitcast_fusion), channel_id=1, source_target_pairs={{8,4},{12,8},{14,12},{10,14},{6,10},{2,6},{0,2},{4,0},{9,5},{13,9}... | collective-permute-start | bytes 786440 | tf_op jit(solution)/shard_map/ppermute | solution.py:143
  94.4 43.6 %collective-permute-start.7 = (bf16[128,1024]{0,1:T(8,128)(2,1)S(1)}, bf16[128,1024]{0,1:T(8,128)(2,1)}, u32[]{:S(2)}, u32[]{:S(2)}) collective-permute-start(bf16[128,1024]{0,1:T(8,128)(2,1)S(1)} %convert_bitcast_fusion), channel_id=1, source_target_pairs={{4,8},{8,12},{12,14},{14,10},{10,6},{6,2},{2,0},{0,4},{5,9},{9,13}... | collective-permute-start | bytes 786440 | tf_op jit(solution)/shard_map/ppermute | solution.py:140
  95.2 1.4 collective-permute-start.14
  98.1 7.0 %collective-permute-start.15 = (f32[128,128]{1,0:T(8,128)S(1)}, f32[128,128]{1,0:T(8,128)S(1)}, u32[]{:S(2)}, u32[]{:S(2)}) collective-permute-start(f32[128,128]{1,0:T(8,128)S(1)} %get-tuple-element.3), channel_id=1, source_target_pairs={{0,2},{2,4},{4,6},{6,8},{8,10},{10,12},{12,14},{14,0},{1,3},{3,5},... | collective-permute-start | bytes 196616 | tf_op jit(solution)/shard_map/ppermute | solution.py:79
  101.6 22.3 %collective-permute-start.20 = (f32[128,128]{1,0:T(8,128)S(1)}, f32[128,128]{1,0:T(8,128)S(1)}, u32[]{:S(2)}, u32[]{:S(2)}) collective-permute-start(f32[128,128]{1,0:T(8,128)S(1)} %get-tuple-element.3), channel_id=1, source_target_pairs={{0,12},{2,14},{4,0},{6,2},{8,4},{10,6},{12,8},{14,10},{1,13},{3,15... | collective-permute-start | bytes 196616 | tf_op jit(solution)/shard_map/ppermute | solution.py:79
  103.0 20.2 %collective-permute-start.19 = (f32[128,128]{1,0:T(8,128)S(1)}, f32[128,128]{1,0:T(8,128)S(1)}, u32[]{:S(2)}, u32[]{:S(2)}) collective-permute-start(f32[128,128]{1,0:T(8,128)S(1)} %get-tuple-element.3), channel_id=1, source_target_pairs={{0,10},{2,12},{4,14},{6,0},{8,2},{10,4},{12,6},{14,8},{1,11},{3,13... | collective-permute-start | bytes 196616 | tf_op jit(solution)/shard_map/ppermute | solution.py:79
  105.0 6.1 %collective-permute-start.16 = (f32[128,128]{1,0:T(8,128)S(1)}, f32[128,128]{1,0:T(8,128)S(1)}, u32[]{:S(2)}, u32[]{:S(2)}) collective-permute-start(f32[128,128]{1,0:T(8,128)S(1)} %get-tuple-element.3), channel_id=1, source_target_pairs={{0,4},{2,6},{4,8},{6,10},{8,12},{10,14},{12,0},{14,2},{1,5},{3,7},... | collective-permute-start | bytes 196616 | tf_op jit(solution)/shard_map/ppermute | solution.py:79
  111.1 6.1 %collective-permute-start.17 = (f32[128,128]{1,0:T(8,128)S(1)}, f32[128,128]{1,0:T(8,128)S(1)}, u32[]{:S(2)}, u32[]{:S(2)}) collective-permute-start(f32[128,128]{1,0:T(8,128)S(1)} %get-tuple-element.3), channel_id=1, source_target_pairs={{0,6},{2,8},{4,10},{6,12},{8,14},{10,0},{12,2},{14,4},{1,7},{3,9},... | collective-permute-start | bytes 196616 | tf_op jit(solution)/shard_map/ppermute | solution.py:79
  117.2 5.4 %collective-permute-start.18 = (f32[128,128]{1,0:T(8,128)S(1)}, f32[128,128]{1,0:T(8,128)S(1)}, u32[]{:S(2)}, u32[]{:S(2)}) collective-permute-start(f32[128,128]{1,0:T(8,128)S(1)} %get-tuple-element.3), channel_id=1, source_target_pairs={{0,8},{2,10},{4,12},{6,14},{8,0},{10,2},{12,4},{14,6},{1,9},{3,11}... | collective-permute-start | bytes 196616 | tf_op jit(solution)/shard_map/ppermute | solution.py:79
  122.6 4.3 %collective-permute-start.21 = (f32[128,128]{1,0:T(8,128)S(1)}, f32[128,128]{1,0:T(8,128)S(1)}, u32[]{:S(2)}, u32[]{:S(2)}) collective-permute-start(f32[128,128]{1,0:T(8,128)S(1)} %get-tuple-element.3), channel_id=1, source_target_pairs={{0,14},{2,0},{4,2},{6,4},{8,6},{10,8},{12,10},{14,12},{1,15},{3,1}... | collective-permute-start | bytes 196616 | tf_op jit(solution)/shard_map/ppermute | solution.py:79
  133.2 5.1 %copy-start.4 = (f32[1024]{0:T(1024)S(1)}, f32[1024]{0:T(1024)}, u32[]{:S(2)}) copy-start(f32[1024]{0:T(1024)} %get-tuple-element.28) | copy-start | bytes 12292
  133.2 5.1 %copy-start.5 = (f32[1024]{0:T(1024)S(1)}, f32[1024]{0:T(1024)}, u32[]{:S(2)}) copy-start(f32[1024]{0:T(1024)} %get-tuple-element.29) | copy-start | bytes 12292
  134.3 5.4 %copy-start.3 = (f32[1024]{0:T(1024)S(1)}, f32[1024]{0:T(1024)}, u32[]{:S(2)}) copy-start(f32[1024]{0:T(1024)} %get-tuple-element.27) | copy-start | bytes 12292
  138.0 8.9 %collective-permute-start.9 = (bf16[128,1024]{0,1:T(8,128)(2,1)}, bf16[128,1024]{0,1:T(8,128)(2,1)S(1)}, u32[]{:S(2)}, u32[]{:S(2)}) collective-permute-start(bf16[128,1024]{0,1:T(8,128)(2,1)} %collective-permute-done.7), channel_id=1, source_target_pairs={{4,8},{8,12},{12,14},{14,10},{10,6},{6,2},{2,0},{0,4},{5,9},{9,13}... | collective-permute-start | bytes 786440 | tf_op jit(solution)/shard_map/ppermute | solution.py:140
  141.3 7.7 %collective-permute-start.10 = (bf16[128,1024]{0,1:T(8,128)(2,1)}, bf16[128,1024]{0,1:T(8,128)(2,1)S(1)}, u32[]{:S(2)}, u32[]{:S(2)}) collective-permute-start(bf16[128,1024]{0,1:T(8,128)(2,1)} %collective-permute-done.8), channel_id=1, source_target_pairs={{8,4},{12,8},{14,12},{10,14},{6,10},{2,6},{0,2},{4,0},{9,5},{13,9}... | collective-permute-start | bytes 786440 | tf_op jit(solution)/shard_map/ppermute | solution.py:143
  146.9 9.2 %collective-permute-start.11 = (bf16[128,1024]{0,1:T(8,128)(2,1)S(1)}, bf16[128,1024]{0,1:T(8,128)(2,1)S(1)}, u32[]{:S(2)}, u32[]{:S(2)}) collective-permute-start(bf16[128,1024]{0,1:T(8,128)(2,1)S(1)} %collective-permute-done.9), channel_id=1, source_target_pairs={{4,8},{8,12},{12,14},{14,10},{10,6},{6,2},{2,0},{0,4},{5,9},{9,13}... | collective-permute-start | bytes 786440 | tf_op jit(solution)/shard_map/ppermute | solution.py:140
  149.0 0.7 copy-start.7
  150.4 6.8 %collective-permute-start.12 = (bf16[128,1024]{0,1:T(8,128)(2,1)}, bf16[128,1024]{0,1:T(8,128)(2,1)S(1)}, u32[]{:S(2)}, u32[]{:S(2)}) collective-permute-start(bf16[128,1024]{0,1:T(8,128)(2,1)} %copy-done.7), channel_id=1, source_target_pairs={{8,4},{12,8},{14,12},{10,14},{6,10},{2,6},{0,2},{4,0},{9,5},{13,9}... | collective-permute-start | bytes 786440 | tf_op jit(solution)/shard_map/ppermute | solution.py:143
  156.1 6.4 %collective-permute-start.13 = (bf16[128,1024]{0,1:T(8,128)(2,1)S(1)}, bf16[128,1024]{0,1:T(8,128)(2,1)S(1)}, u32[]{:S(2)}, u32[]{:S(2)}) collective-permute-start(bf16[128,1024]{0,1:T(8,128)(2,1)S(1)} %collective-permute-done.11), channel_id=1, source_target_pairs={{4,8},{8,12},{12,14},{14,10},{10,6},{6,2},{2,0},{0,4},{5,9},{9,13}... | collective-permute-start | bytes 786440 | tf_op jit(solution)/shard_map/ppermute | solution.py:140
where the time goes:
time: 165 us; the launch traced here: 164 us
  waiting for transfers between devices  49.3 us (30%)
  local copies, waits for them, and re-layouts  30.2 us (18%)
  other arithmetic  27.9 us (17%)
  starting transfers between devices  27.7 us (17%)
  matrix products  16.9 us (10%)
  between operations  11.7 us (7%)
    ppermute x14, waiting for transfers between devices, gather_blocks(): received.append(lax.ppermute(block, axis, pairs))  29 us
    ppermute x14, starting transfers between devices, gather_blocks(): received.append(lax.ppermute(block, axis, pairs))  16.8 us
    another operation x3, other arithmetic, invert(): factor = jnp.linalg.cholesky(matrix)  12.4 us
    another operation x2, other arithmetic, invert(): lax.linalg.triangular_solve(factor, identity, left_side=True, lower=True)  10.5 us
    all_to_all x1, waiting for transfers between devices, per_device(): expression_genes = lax.all_to_all(sent, 'cell', 1, 0, tiled=True)  9.38 us
    unnamed x32, local copies, waits for them, and re-layouts  8.62 us
    dot_general x26, matrix products, matmul(): return jnp.dot(left, right, precision=lax.Precision.HIGHEST)  8.15 us
    ppermute x4, waiting for transfers between devices, per_device(): ahead = lax.ppermute(ahead, 'cell', forward)  7.9 us
  transfers between devices with their start and end apart: 23, of which 15 were waited for; matrix products, arithmetic and copies ran while one was open for 36% of the time, Pallas kernels for 0%

commit v1 on v0

--- a/solution.py
+++ b/solution.py
@@ -7,6 +7,29 @@
 
 NS_STEPS = 8
 shrink_rate = 0.25
+
+
+def split_up(array, dim, size):
+    dims = array.shape
+    pieces = array.reshape(*dims[:dim], size, dims[dim] // size, *dims[dim + 1 :])
+    return jnp.moveaxis(pieces, dim, 0)
+
+
+def joined_along(tiles, dim):
+    shape = list(tiles.shape[1:])
+    shape[dim] *= tiles.shape[0]
+    return jnp.moveaxis(tiles, 0, dim).reshape(shape)
+
+
+def swapped_with_each(shard, axis, split_dim, concat_dim):
+    count, index = (lax.axis_size(axis), lax.axis_index(axis))
+    pieces = split_up(shard, split_dim, count)
+    outs = [pieces[index]]
+    for step in range(1, count):
+        sent = pieces[index ^ step]
+        outs.append(lax.ppermute(sent, axis, [(i, i ^ step) for i in range(count)]))
+    pieces = jnp.stack(outs)[index ^ jnp.arange(count)]
+    return joined_along(pieces, concat_dim)
 
 
 def matmul(left, right):
@@ -100,7 +123,7 @@
     identity = jnp.eye(width, dtype=jnp.float32)
     design_all = gather_blocks(design, "cell").reshape(-1, width)
     sent = expression + (design_all[0, 0] * 0).astype(expression.dtype)
-    expression_genes = lax.all_to_all(sent, "cell", 1, 0, tiled=True)
+    expression_genes = swapped_with_each(sent, "cell", 1, 0)
     gram_total = lax.dot_general(
         design_all, design_all, (((0,), (0,)), ((), ())), preferred_element_type=jnp.float32
     )

time: 165 us -> 172 us (1.042)
  waiting for transfers between devices: 49.3 us -> 19.2 us
  starting transfers between devices: 27.7 us -> 49.1 us
  local copies, waits for them, and re-layouts: 30.2 us -> 47.2 us
    ppermute x14, waiting for transfers between devices: 29 us -> 8.58 us  [gather_blocks(): received.append(lax.ppermute(block, axis, pairs))]
    ppermute x0 -> x7, starting transfers between devices: none -> 11.3 us  [swapped_with_each(): outs.append(lax.ppermute(sent, axis, [(i, i ^ step) for i in range(count)]))]
    another operation x0 -> x10, local copies, waits for them, and re-layouts: none -> 9.85 us
    unnamed x32 -> x47, local copies, waits for them, and re-layouts: 8.62 us -> 18.4 us
    all_to_all x1 -> x0, waiting for transfers between devices: 9.38 us -> none  [per_device(): expression_genes = lax.all_to_all(sent, 'cell', 1, 0, tiled=True)]
    ppermute x14, starting transfers between devices: 16.8 us -> 25.3 us  [gather_blocks(): received.append(lax.ppermute(block, axis, pairs))]
    all_to_all x2 -> x0, local copies, waits for them, and re-layouts: 7.81 us -> none  [per_device(): expression_genes = lax.all_to_all(sent, 'cell', 1, 0, tiled=True)]
    ppermute x4, starting transfers between devices: 1.28 us -> 8.06 us  [per_device(): ahead = lax.ppermute(ahead, 'cell', forward)]
  transfers between devices with their start and end apart: 23 -> 29, of which waited for: 15 -> 12; matrix products, arithmetic and copies ran while one was open for 36% -> 43% of each run, Pallas kernels for 0% -> 0%
where the time goes in v1:
time: 172 us; the launch traced here: 171 us
  starting transfers between devices  49.1 us (29%)
  local copies, waits for them, and re-layouts  47.2 us (27%)
  other arithmetic  26.6 us (15%)
  waiting for transfers between devices  19.2 us (11%)
  matrix products  16.9 us (10%)
  between operations  11.8 us (7%)
    ppermute x14, starting transfers between devices, gather_blocks(): received.append(lax.ppermute(block, axis, pairs))  25.3 us
    unnamed x47, local copies, waits for them, and re-layouts  18.4 us
    another operation x3, other arithmetic, invert(): factor = jnp.linalg.cholesky(matrix)  12.4 us
    ppermute x7, starting transfers between devices, swapped_with_each(): outs.append(lax.ppermute(sent, axis, [(i, i ^ step) for i in range(count)]))  11.3 us
    another operation x2, other arithmetic, invert(): lax.linalg.triangular_solve(factor, identity, left_side=True, lower=True)  10.4 us
    another operation x9, local copies, waits for them, and re-layouts  9.13 us
    ppermute x14, waiting for transfers between devices, gather_blocks(): received.append(lax.ppermute(block, axis, pairs))  8.58 us
    dot_general x26, matrix products, matmul(): return jnp.dot(left, right, precision=lax.Precision.HIGHEST)  8.14 us
  transfers between devices with their start and end apart: 29, of which 12 were waited for; matrix products, arithmetic and copies ran while one was open for 43% of the time, Pallas kernels for 0%

profile of v1, /device:TPU:0, one launch (start us, length us, event | category | flops | bytes accessed | tf_op | source)
XLA Modules:
  0.0 170.8 jit_solution(10292764795907207086)
XLA Ops:
  0.6 3.0 %collective-permute-start = (bf16[128,128]{1,0:T(8,128)(2,1)}, bf16[128,128]{1,0:T(8,128)(2,1)S(1)}, u32[]{:S(2)}, u32[]{:S(2)}) collective-permute-start(bf16[128,128]{1,0:T(8,128)(2,1)} %param.6), channel_id=1, source_target_pairs={{0,2},{2,4},{4,6},{6,8},{8,10},{10,12},{12,14},{14,0},{1,3},{3,5},... | collective-permute-start | bytes 98312 | tf_op jit(solution)/shard_map/ppermute | solution.py:102
  3.6 1.6 collective-permute-start.1
  5.2 2.6 %collective-permute-start.2 = (bf16[128,128]{1,0:T(8,128)(2,1)}, bf16[128,128]{1,0:T(8,128)(2,1)S(1)}, u32[]{:S(2)}, u32[]{:S(2)}) collective-permute-start(bf16[128,128]{1,0:T(8,128)(2,1)} %param.6), channel_id=1, source_target_pairs={{0,6},{2,8},{4,10},{6,12},{8,14},{10,0},{12,2},{14,4},{1,7},{3,9},... | collective-permute-start | bytes 98312 | tf_op jit(solution)/shard_map/ppermute | solution.py:102
  7.8 1.2 collective-permute-start.3
  9.0 2.6 %collective-permute-start.4 = (bf16[128,128]{1,0:T(8,128)(2,1)}, bf16[128,128]{1,0:T(8,128)(2,1)S(1)}, u32[]{:S(2)}, u32[]{:S(2)}) collective-permute-start(bf16[128,128]{1,0:T(8,128)(2,1)} %param.6), channel_id=1, source_target_pairs={{0,10},{2,12},{4,14},{6,0},{8,2},{10,4},{12,6},{14,8},{1,11},{3,13... | collective-permute-start | bytes 98312 | tf_op jit(solution)/shard_map/ppermute | solution.py:102
  11.6 0.8 constant_dynamic-update-slice_fusion.7
  12.5 1.2 dynamic_slice.85
  18.4 1.6 fusion.31
  24.6 1.4 broadcast_add_fusion.1
  26.5 3.2 %copy.43 = bf16[128,8192]{0,1:T(8,128)(2,1)S(1)} copy(bf16[128,8192]{1,0:T(8,128)(2,1)} %param.5) | data formatting | bytes 4194304 | tf_op args[0]
  29.8 1.4 collective-permute-start.5
  31.2 1.5 collective-permute-start.6
  32.8 1.0 collective-permute-done.5
  33.8 1.4 collective-permute-done.6
  38.2 0.9 constant_dynamic-slice_fusion
  39.1 1.8 %copy.45 = bf16[128,1,1024]{2,0,1:T(8,128)(2,1)} copy(bf16[128,1,1024]{0,2,1:T(8,128)(2,1)} %get-tuple-element.27) | data formatting | bytes 524288 | tf_op jit(solution)/shard_map/dynamic-slice
  40.9 1.7 bitcast_dynamic-update-slice_fusion.7
  42.6 1.8 %copy.46 = bf16[128,1,1024]{2,0,1:T(8,128)(2,1)} copy(bf16[128,1,1024]{0,2,1:T(8,128)(2,1)} %get-tuple-element.26) | data formatting | bytes 524288 | tf_op jit(solution)/shard_map/dynamic-slice.1
  44.3 1.5 collective-permute-start.7
  45.9 1.8 %copy.47 = bf16[128,1,1024]{2,0,1:T(8,128)(2,1)} copy(bf16[128,1,1024]{0,2,1:T(8,128)(2,1)} %get-tuple-element.25) | data formatting | bytes 524288 | tf_op jit(solution)/shard_map/dynamic-slice.2
  47.8 0.8 copy.48
  48.6 1.8 %collective-permute-start.9 = (bf16[128,1024]{1,0:T(8,128)(2,1)}, bf16[128,1024]{1,0:T(8,128)(2,1)}, u32[]{:S(2)}, u32[]{:S(2)}) collective-permute-start(bf16[128,1024]{1,0:T(8,128)(2,1)} %bitcast.214), channel_id=1, source_target_pairs={{0,6},{2,4},{4,2},{6,0},{8,14},{10,12},{12,10},{14,8},{1,7},{3,5},... | collective-permute-start | bytes 786440 | tf_op jit(solution)/shard_map/ppermute | solution.py:30
  50.5 0.8 copy.49
  51.3 1.8 %collective-permute-start.10 = (bf16[128,1024]{1,0:T(8,128)(2,1)}, bf16[128,1024]{1,0:T(8,128)(2,1)}, u32[]{:S(2)}, u32[]{:S(2)}) collective-permute-start(bf16[128,1024]{1,0:T(8,128)(2,1)} %bitcast.20), channel_id=1, source_target_pairs={{0,8},{2,10},{4,12},{6,14},{8,0},{10,2},{12,4},{14,6},{1,9},{3,11}... | collective-permute-start | bytes 786440 | tf_op jit(solution)/shard_map/ppermute | solution.py:30
  53.2 2.2 %collective-permute-start.11 = (bf16[128,1024]{1,0:T(8,128)(2,1)S(1)}, bf16[128,1024]{1,0:T(8,128)(2,1)S(1)}, u32[]{:S(2)}, u32[]{:S(2)}) collective-permute-start(bf16[128,1024]{1,0:T(8,128)(2,1)S(1)} %bitcast.213), channel_id=1, source_target_pairs={{0,10},{2,8},{4,14},{6,12},{8,2},{10,0},{12,6},{14,4},{1,11},{3,9}... | collective-permute-start | bytes 786440 | tf_op jit(solution)/shard_map/ppermute | solution.py:30
  55.6 11.7 %cholesky.29 = f32[128,128]{1,0:T(8,128)S(1)} custom-call(f32[128,128]{1,0:T(8,128)S(1)} %fusion.22), custom_call_target="Cholesky" | custom-call | tf_op jit(solution)/shard_map/jit(cholesky)/cholesky | solution.py:41
  68.5 9.8 %custom-call.6 = f32[1,128,128]{1,2,0:T(8,128)S(1)} custom-call(f32[1,128,128]{2,1,0:T(8,128)S(1)} %fusion.18), custom_call_target="InvertDiagBlocksLowerTriangular" | custom-call | tf_op jit(solution)/shard_map/triangular_solve | solution.py:42
  78.9 0.9 copy.51
  79.9 3.2 %collective-permute-start.12 = (bf16[128,1024]{1,0:T(8,128)(2,1)}, bf16[128,1024]{1,0:T(8,128)(2,1)S(1)}, u32[]{:S(2)}, u32[]{:S(2)}) collective-permute-start(bf16[128,1024]{1,0:T(8,128)(2,1)} %bitcast.218), channel_id=1, source_target_pairs={{0,12},{2,14},{4,8},{6,10},{8,4},{10,6},{12,0},{14,2},{1,13},{3,15... | collective-permute-start | bytes 786440 | tf_op jit(solution)/shard_map/ppermute | solution.py:30
  83.1 1.7 bitcast_dynamic-update-slice_fusion.6
  85.4 1.7 bitcast_dynamic-update-slice_fusion.5
  87.1 1.7 bitcast_dynamic-update-slice_fusion.4
  88.7 1.7 bitcast_dynamic-update-slice_fusion.3
  91.9 2.1 %collective-permute-done.13 = bf16[128,1024]{1,0:T(8,128)(2,1)S(1)} collective-permute-done((bf16[128,1024]{1,0:T(8,128)(2,1)S(1)}, bf16[128,1024]{1,0:T(8,128)(2,1)S(1)}, u32[]{:S(2)}, u32[]{:S(2)}) %collective-permute-start.13) | collective-permute-done | bytes 262176 | tf_op jit(solution)/shard_map/ppermute | solution.py:30
  94.7 3.7 %gather_fusion.1 = bf16[8,128,1024]{2,1,0:T(8,128)(2,1)} fusion(bf16[8,128,1024]{2,1,0:T(8,128)(2,1)} %bitcast_dynamic-update-slice_fusion, s32[1024]{0:T(1024)S(1)} %pad_clamp_fusion), kind=kCustom, calls=%fused_computation.1 | custom fusion | bytes 4194336 | tf_op jit(solution)/shard_map/gather | solution.py:31
  98.3 2.4 %convolution_bitcast_fusion.8 = f32[1024,128]{1,0:T(8,128)S(1)} fusion(bf16[8,128,1024]{2,1,0:T(8,128)(2,1)} %gather_fusion.1, bf16[8,128,128]{2,1,0:T(8,128)(2,1)S(1)} %copy-done.1, pred[8]{0:T(512)(128)(4,1)S(1)} %copy-done.10), kind=kOutput, calls=%fused_computation.19 | convolution fusion | flops 268566528 | bytes 2883592 | tf_op jit(solution)/shard_map/dot_general | solution.py:131
  101.3 1.0 fusion.34
  102.4 8.1 %collective-permute-start.14 = (bf16[128,1024]{0,1:T(8,128)(2,1)S(1)}, bf16[128,1024]{0,1:T(8,128)(2,1)}, u32[]{:S(2)}, u32[]{:S(2)}) collective-permute-start(bf16[128,1024]{0,1:T(8,128)(2,1)S(1)} %convert_bitcast_fusion), channel_id=1, source_target_pairs={{4,8},{8,12},{12,14},{14,10},{10,6},{6,2},{2,0},{0,4},{5,9},{9,13}... | collective-permute-start | bytes 786440 | tf_op jit(solution)/shard_map/ppermute | solution.py:163
  110.9 0.9 collective-permute-done.21
  111.8 1.5 bitcast_dynamic-update-slice_fusion.15
  113.3 1.7 collective-permute-start.22
  115.0 1.5 broadcast_in_dim.42
  117.2 1.8 %collective-permute-start.23 = (f32[128,128]{1,0:T(8,128)S(1)}, f32[128,128]{1,0:T(8,128)S(1)}, u32[]{:S(2)}, u32[]{:S(2)}) collective-permute-start(f32[128,128]{1,0:T(8,128)S(1)} %get-tuple-element.3), channel_id=1, source_target_pairs={{0,4},{2,6},{4,8},{6,10},{8,12},{10,14},{12,0},{14,2},{1,5},{3,7},... | collective-permute-start | bytes 196616 | tf_op jit(solution)/shard_map/ppermute | solution.py:102
  119.0 1.2 collective-permute-start.24
  120.2 2.6 %collective-permute-start.25 = (f32[128,128]{1,0:T(8,128)S(1)}, f32[128,128]{1,0:T(8,128)S(1)}, u32[]{:S(2)}, u32[]{:S(2)}) collective-permute-start(f32[128,128]{1,0:T(8,128)S(1)} %get-tuple-element.3), channel_id=1, source_target_pairs={{0,8},{2,10},{4,12},{6,14},{8,0},{10,2},{12,4},{14,6},{1,9},{3,11}... | collective-permute-start | bytes 196616 | tf_op jit(solution)/shard_map/ppermute | solution.py:102
  123.5 0.9 collective-permute-start.26
  125.0 3.8 %collective-permute-done.24 = f32[128,128]{1,0:T(8,128)S(1)} collective-permute-done((f32[128,128]{1,0:T(8,128)S(1)}, f32[128,128]{1,0:T(8,128)S(1)}, u32[]{:S(2)}, u32[]{:S(2)}) %collective-permute-start.24) | collective-permute-done | bytes 65568 | tf_op jit(solution)/shard_map/ppermute | solution.py:102
  128.8 3.2 %collective-permute-start.27 = (f32[128,128]{1,0:T(8,128)S(1)}, f32[128,128]{1,0:T(8,128)S(1)}, u32[]{:S(2)}, u32[]{:S(2)}) collective-permute-start(f32[128,128]{1,0:T(8,128)S(1)} %get-tuple-element.3), channel_id=1, source_target_pairs={{0,12},{2,14},{4,0},{6,2},{8,4},{10,6},{12,8},{14,10},{1,13},{3,15... | collective-permute-start | bytes 196616 | tf_op jit(solution)/shard_map/ppermute | solution.py:102
  134.7 2.2 %collective-permute-done.28 = f32[128,128]{1,0:T(8,128)S(1)} collective-permute-done((f32[128,128]{1,0:T(8,128)S(1)}, f32[128,128]{1,0:T(8,128)S(1)}, u32[]{:S(2)}, u32[]{:S(2)}) %collective-permute-start.28) | collective-permute-done | bytes 65568 | tf_op jit(solution)/shard_map/ppermute | solution.py:102
  137.5 1.6 gather_fusion.2
  139.9 0.8 fusion.16
  140.7 0.8 fusion.24
  146.1 1.4 fusion.8
  147.5 1.3 subtract_convert_fusion.6
  148.8 1.3 subtract_convert_fusion.5
  150.4 2.1 %collective-permute-start.17 = (bf16[128,1024]{0,1:T(8,128)(2,1)}, bf16[128,1024]{0,1:T(8,128)(2,1)S(1)}, u32[]{:S(2)}, u32[]{:S(2)}) collective-permute-start(bf16[128,1024]{0,1:T(8,128)(2,1)} %collective-permute-done.15), channel_id=1, source_target_pairs={{8,4},{12,8},{14,12},{10,14},{6,10},{2,6},{0,2},{4,0},{9,5},{13,9}... | collective-permute-start | bytes 786440 | tf_op jit(solution)/shard_map/ppermute | solution.py:166
  154.0 1.2 collective-permute-done.16
  155.5 1.6 collective-permute-done.17
  158.4 2.4 %collective-permute-start.19 = (bf16[128,1024]{0,1:T(8,128)(2,1)}, bf16[128,1024]{0,1:T(8,128)(2,1)S(1)}, u32[]{:S(2)}, u32[]{:S(2)}) collective-permute-start(bf16[128,1024]{0,1:T(8,128)(2,1)} %copy-done.12), channel_id=1, source_target_pairs={{8,4},{12,8},{14,12},{10,14},{6,10},{2,6},{0,2},{4,0},{9,5},{13,9}... | collective-permute-start | bytes 786440 | tf_op jit(solution)/shard_map/ppermute | solution.py:166
  162.2 1.0 collective-permute-done.18
  163.6 1.5 collective-permute-done.19
  165.7 0.7 constant_dynamic-update-slice_fusion.10
  167.2 2.4 %collective-permute-done.20 = bf16[128,1024]{0,1:T(8,128)(2,1)S(1)} collective-permute-done((bf16[128,1024]{0,1:T(8,128)(2,1)S(1)}, bf16[128,1024]{0,1:T(8,128)(2,1)S(1)}, u32[]{:S(2)}, u32[]{:S(2)}) %collective-permute-start.20) | collective-permute-done | bytes 262176 | tf_op jit(solution)/shard_map/ppermute | solution.py:163
  170.1 0.7 constant_dynamic-update-slice_fusion.8
  (134 shorter events, 26.0 us)
Async XLA Ops:
  0.6 29.2 %collective-permute-start = (bf16[128,128]{1,0:T(8,128)(2,1)}, bf16[128,128]{1,0:T(8,128)(2,1)S(1)}, u32[]{:S(2)}, u32[]{:S(2)}) collective-permute-start(bf16[128,128]{1,0:T(8,128)(2,1)} %param.6), channel_id=1, source_target_pairs={{0,2},{2,4},{4,6},{6,8},{8,10},{10,12},{12,14},{14,0},{1,3},{3,5},... | collective-permute-start | bytes 98312 | tf_op jit(solution)/shard_map/ppermute | solution.py:102
  3.6 27.6 %collective-permute-start.1 = (bf16[128,128]{1,0:T(8,128)(2,1)}, bf16[128,128]{1,0:T(8,128)(2,1)S(1)}, u32[]{:S(2)}, u32[]{:S(2)}) collective-permute-start(bf16[128,128]{1,0:T(8,128)(2,1)} %param.6), channel_id=1, source_target_pairs={{0,4},{2,6},{4,8},{6,10},{8,12},{10,14},{12,0},{14,2},{1,5},{3,7},... | collective-permute-start | bytes 98312 | tf_op jit(solution)/shard_map/ppermute | solution.py:102
  5.2 27.5 %collective-permute-start.2 = (bf16[128,128]{1,0:T(8,128)(2,1)}, bf16[128,128]{1,0:T(8,128)(2,1)S(1)}, u32[]{:S(2)}, u32[]{:S(2)}) collective-permute-start(bf16[128,128]{1,0:T(8,128)(2,1)} %param.6), channel_id=1, source_target_pairs={{0,6},{2,8},{4,10},{6,12},{8,14},{10,0},{12,2},{14,4},{1,7},{3,9},... | collective-permute-start | bytes 98312 | tf_op jit(solution)/shard_map/ppermute | solution.py:102
  7.8 25.0 %collective-permute-start.3 = (bf16[128,128]{1,0:T(8,128)(2,1)}, bf16[128,128]{1,0:T(8,128)(2,1)S(1)}, u32[]{:S(2)}, u32[]{:S(2)}) collective-permute-start(bf16[128,128]{1,0:T(8,128)(2,1)} %param.6), channel_id=1, source_target_pairs={{0,8},{2,10},{4,12},{6,14},{8,0},{10,2},{12,4},{14,6},{1,9},{3,11}... | collective-permute-start | bytes 98312 | tf_op jit(solution)/shard_map/ppermute | solution.py:102
  9.0 23.8 %collective-permute-start.4 = (bf16[128,128]{1,0:T(8,128)(2,1)}, bf16[128,128]{1,0:T(8,128)(2,1)S(1)}, u32[]{:S(2)}, u32[]{:S(2)}) collective-permute-start(bf16[128,128]{1,0:T(8,128)(2,1)} %param.6), channel_id=1, source_target_pairs={{0,10},{2,12},{4,14},{6,0},{8,2},{10,4},{12,6},{14,8},{1,11},{3,13... | collective-permute-start | bytes 98312 | tf_op jit(solution)/shard_map/ppermute | solution.py:102
  12.5 23.3 %copy-start.9 = (pred[8]{0:T(512)(128)(4,1)}, pred[8]{0:T(512)(128)(4,1)S(1)}, u32[]{:S(2)}) copy-start(pred[8]{0:T(512)(128)(4,1)S(1)} %compare_and_fusion) | copy-start | bytes 28
  26.5 3.3 %copy-start.2 = (bf16[128,128]{1,0:T(8,128)(2,1)S(1)}, bf16[128,128]{1,0:T(8,128)(2,1)}, u32[]{:S(2)}) copy-start(bf16[128,128]{1,0:T(8,128)(2,1)} %param.6) | copy-start | bytes 98308
  29.8 4.0 %collective-permute-start.5 = (bf16[128,128]{1,0:T(8,128)(2,1)S(1)}, bf16[128,128]{1,0:T(8,128)(2,1)S(1)}, u32[]{:S(2)}, u32[]{:S(2)}) collective-permute-start(bf16[128,128]{1,0:T(8,128)(2,1)S(1)} %copy-done.2), channel_id=1, source_target_pairs={{0,12},{2,14},{4,0},{6,2},{8,4},{10,6},{12,8},{14,10},{1,13},{3,15... | collective-permute-start | bytes 98312 | tf_op jit(solution)/shard_map/ppermute | solution.py:102
  31.2 4.0 %collective-permute-start.6 = (bf16[128,128]{1,0:T(8,128)(2,1)S(1)}, bf16[128,128]{1,0:T(8,128)(2,1)S(1)}, u32[]{:S(2)}, u32[]{:S(2)}) collective-permute-start(bf16[128,128]{1,0:T(8,128)(2,1)S(1)} %copy-done.2), channel_id=1, source_target_pairs={{0,14},{2,0},{4,2},{6,4},{8,6},{10,8},{12,10},{14,12},{1,15},{3,1}... | collective-permute-start | bytes 98312 | tf_op jit(solution)/shard_map/ppermute | solution.py:102
  35.8 2.3 %copy-start = (bf16[8,128,128]{2,1,0:T(8,128)(2,1)}, bf16[8,128,128]{2,1,0:T(8,128)(2,1)S(1)}, u32[]{:S(2)}) copy-start(bf16[8,128,128]{2,1,0:T(8,128)(2,1)S(1)} %gather_fusion) | copy-start | bytes 786436
  44.3 35.6 %collective-permute-start.7 = (bf16[128,1024]{1,0:T(8,128)(2,1)}, bf16[128,1024]{1,0:T(8,128)(2,1)}, u32[]{:S(2)}, u32[]{:S(2)}) collective-permute-start(bf16[128,1024]{1,0:T(8,128)(2,1)} %bitcast.216), channel_id=1, source_target_pairs={{0,2},{2,0},{4,6},{6,4},{8,10},{10,8},{12,14},{14,12},{1,3},{3,1},... | collective-permute-start | bytes 786440 | tf_op jit(solution)/shard_map/ppermute | solution.py:30
  47.7 37.1 %collective-permute-start.8 = (bf16[128,1024]{1,0:T(8,128)(2,1)}, bf16[128,1024]{1,0:T(8,128)(2,1)}, u32[]{:S(2)}, u32[]{:S(2)}) collective-permute-start(bf16[128,1024]{1,0:T(8,128)(2,1)} %bitcast.215), channel_id=1, source_target_pairs={{0,4},{2,6},{4,0},{6,2},{8,12},{10,14},{12,8},{14,10},{1,5},{3,7},... | collective-permute-start | bytes 786440 | tf_op jit(solution)/shard_map/ppermute | solution.py:30
  48.6 38.4 %collective-permute-start.9 = (bf16[128,1024]{1,0:T(8,128)(2,1)}, bf16[128,1024]{1,0:T(8,128)(2,1)}, u32[]{:S(2)}, u32[]{:S(2)}) collective-permute-start(bf16[128,1024]{1,0:T(8,128)(2,1)} %bitcast.214), channel_id=1, source_target_pairs={{0,6},{2,4},{4,2},{6,0},{8,14},{10,12},{12,10},{14,8},{1,7},{3,5},... | collective-permute-start | bytes 786440 | tf_op jit(solution)/shard_map/ppermute | solution.py:30
  51.3 37.4 %collective-permute-start.10 = (bf16[128,1024]{1,0:T(8,128)(2,1)}, bf16[128,1024]{1,0:T(8,128)(2,1)}, u32[]{:S(2)}, u32[]{:S(2)}) collective-permute-start(bf16[128,1024]{1,0:T(8,128)(2,1)} %bitcast.20), channel_id=1, source_target_pairs={{0,8},{2,10},{4,12},{6,14},{8,0},{10,2},{12,4},{14,6},{1,9},{3,11}... | collective-permute-start | bytes 786440 | tf_op jit(solution)/shard_map/ppermute | solution.py:30
  53.2 37.2 %collective-permute-start.11 = (bf16[128,1024]{1,0:T(8,128)(2,1)S(1)}, bf16[128,1024]{1,0:T(8,128)(2,1)S(1)}, u32[]{:S(2)}, u32[]{:S(2)}) collective-permute-start(bf16[128,1024]{1,0:T(8,128)(2,1)S(1)} %bitcast.213), channel_id=1, source_target_pairs={{0,10},{2,8},{4,14},{6,12},{8,2},{10,0},{12,6},{14,4},{1,11},{3,9}... | collective-permute-start | bytes 786440 | tf_op jit(solution)/shard_map/ppermute | solution.py:30
  79.9 11.2 %collective-permute-start.12 = (bf16[128,1024]{1,0:T(8,128)(2,1)}, bf16[128,1024]{1,0:T(8,128)(2,1)S(1)}, u32[]{:S(2)}, u32[]{:S(2)}) collective-permute-start(bf16[128,1024]{1,0:T(8,128)(2,1)} %bitcast.218), channel_id=1, source_target_pairs={{0,12},{2,14},{4,8},{6,10},{8,4},{10,6},{12,0},{14,2},{1,13},{3,15... | collective-permute-start | bytes 786440 | tf_op jit(solution)/shard_map/ppermute | solution.py:30
  84.8 9.1 %collective-permute-start.13 = (bf16[128,1024]{1,0:T(8,128)(2,1)S(1)}, bf16[128,1024]{1,0:T(8,128)(2,1)S(1)}, u32[]{:S(2)}, u32[]{:S(2)}) collective-permute-start(bf16[128,1024]{1,0:T(8,128)(2,1)S(1)} %bitcast.217), channel_id=1, source_target_pairs={{0,14},{2,12},{4,10},{6,8},{8,6},{10,4},{12,2},{14,0},{1,15},{3,13... | collective-permute-start | bytes 786440 | tf_op jit(solution)/shard_map/ppermute | solution.py:30
  94.7 3.7 %copy-start.1 = (bf16[8,128,128]{2,1,0:T(8,128)(2,1)S(1)}, bf16[8,128,128]{2,1,0:T(8,128)(2,1)}, u32[]{:S(2)}) copy-start(bf16[8,128,128]{2,1,0:T(8,128)(2,1)} %copy-done) | copy-start | bytes 786436
  94.7 3.7 %copy-start.10 = (pred[8]{0:T(512)(128)(4,1)S(1)}, pred[8]{0:T(512)(128)(4,1)}, u32[]{:S(2)}) copy-start(pred[8]{0:T(512)(128)(4,1)} %copy-done.9) | copy-start | bytes 28
  102.4 45.1 %collective-permute-start.14 = (bf16[128,1024]{0,1:T(8,128)(2,1)S(1)}, bf16[128,1024]{0,1:T(8,128)(2,1)}, u32[]{:S(2)}, u32[]{:S(2)}) collective-permute-start(bf16[128,1024]{0,1:T(8,128)(2,1)S(1)} %convert_bitcast_fusion), channel_id=1, source_target_pairs={{4,8},{8,12},{12,14},{14,10},{10,6},{6,2},{2,0},{0,4},{5,9},{9,13}... | collective-permute-start | bytes 786440 | tf_op jit(solution)/shard_map/ppermute | solution.py:163
  110.4 38.4 %collective-permute-start.15 = (bf16[128,1024]{0,1:T(8,128)(2,1)S(1)}, bf16[128,1024]{0,1:T(8,128)(2,1)}, u32[]{:S(2)}, u32[]{:S(2)}) collective-permute-start(bf16[128,1024]{0,1:T(8,128)(2,1)S(1)} %convert_bitcast_fusion), channel_id=1, source_target_pairs={{8,4},{12,8},{14,12},{10,14},{6,10},{2,6},{0,2},{4,0},{9,5},{13,9}... | collective-permute-start | bytes 786440 | tf_op jit(solution)/shard_map/ppermute | solution.py:166
  110.4 1.4 collective-permute-start.21
  113.3 25.9 %copy-start.11 = (pred[8]{0:T(512)(128)(4,1)S(1)}, pred[8]{0:T(512)(128)(4,1)}, u32[]{:S(2)}) copy-start(pred[8]{0:T(512)(128)(4,1)} %copy-done.9) | copy-start | bytes 28
  113.3 7.0 %collective-permute-start.22 = (f32[128,128]{1,0:T(8,128)S(1)}, f32[128,128]{1,0:T(8,128)S(1)}, u32[]{:S(2)}, u32[]{:S(2)}) collective-permute-start(f32[128,128]{1,0:T(8,128)S(1)} %get-tuple-element.3), channel_id=1, source_target_pairs={{0,2},{2,4},{4,6},{6,8},{8,10},{10,12},{12,14},{14,0},{1,3},{3,5},... | collective-permute-start | bytes 196616 | tf_op jit(solution)/shard_map/ppermute | solution.py:102
  117.2 6.3 %collective-permute-start.23 = (f32[128,128]{1,0:T(8,128)S(1)}, f32[128,128]{1,0:T(8,128)S(1)}, u32[]{:S(2)}, u32[]{:S(2)}) collective-permute-start(f32[128,128]{1,0:T(8,128)S(1)} %get-tuple-element.3), channel_id=1, source_target_pairs={{0,4},{2,6},{4,8},{6,10},{8,12},{10,14},{12,0},{14,2},{1,5},{3,7},... | collective-permute-start | bytes 196616 | tf_op jit(solution)/shard_map/ppermute | solution.py:102
  119.0 9.8 %collective-permute-start.24 = (f32[128,128]{1,0:T(8,128)S(1)}, f32[128,128]{1,0:T(8,128)S(1)}, u32[]{:S(2)}, u32[]{:S(2)}) collective-permute-start(f32[128,128]{1,0:T(8,128)S(1)} %get-tuple-element.3), channel_id=1, source_target_pairs={{0,6},{2,8},{4,10},{6,12},{8,14},{10,0},{12,2},{14,4},{1,7},{3,9},... | collective-permute-start | bytes 196616 | tf_op jit(solution)/shard_map/ppermute | solution.py:102
  120.2 12.4 %collective-permute-start.25 = (f32[128,128]{1,0:T(8,128)S(1)}, f32[128,128]{1,0:T(8,128)S(1)}, u32[]{:S(2)}, u32[]{:S(2)}) collective-permute-start(f32[128,128]{1,0:T(8,128)S(1)} %get-tuple-element.3), channel_id=1, source_target_pairs={{0,8},{2,10},{4,12},{6,14},{8,0},{10,2},{12,4},{14,6},{1,9},{3,11}... | collective-permute-start | bytes 196616 | tf_op jit(solution)/shard_map/ppermute | solution.py:102
  123.5 9.9 %collective-permute-start.26 = (f32[128,128]{1,0:T(8,128)S(1)}, f32[128,128]{1,0:T(8,128)S(1)}, u32[]{:S(2)}, u32[]{:S(2)}) collective-permute-start(f32[128,128]{1,0:T(8,128)S(1)} %get-tuple-element.3), channel_id=1, source_target_pairs={{0,10},{2,12},{4,14},{6,0},{8,2},{10,4},{12,6},{14,8},{1,11},{3,13... | collective-permute-start | bytes 196616 | tf_op jit(solution)/shard_map/ppermute | solution.py:102
  128.8 5.2 %collective-permute-start.27 = (f32[128,128]{1,0:T(8,128)S(1)}, f32[128,128]{1,0:T(8,128)S(1)}, u32[]{:S(2)}, u32[]{:S(2)}) collective-permute-start(f32[128,128]{1,0:T(8,128)S(1)} %get-tuple-element.3), channel_id=1, source_target_pairs={{0,12},{2,14},{4,0},{6,2},{8,4},{10,6},{12,8},{14,10},{1,13},{3,15... | collective-permute-start | bytes 196616 | tf_op jit(solution)/shard_map/ppermute | solution.py:102
  132.6 4.3 %collective-permute-start.28 = (f32[128,128]{1,0:T(8,128)S(1)}, f32[128,128]{1,0:T(8,128)S(1)}, u32[]{:S(2)}, u32[]{:S(2)}) collective-permute-start(f32[128,128]{1,0:T(8,128)S(1)} %get-tuple-element.3), channel_id=1, source_target_pairs={{0,14},{2,0},{4,2},{6,4},{8,6},{10,8},{12,10},{14,12},{1,15},{3,1}... | collective-permute-start | bytes 196616 | tf_op jit(solution)/shard_map/ppermute | solution.py:102
  142.6 4.8 %copy-start.7 = (f32[1024]{0:T(1024)S(1)}, f32[1024]{0:T(1024)}, u32[]{:S(2)}) copy-start(f32[1024]{0:T(1024)} %get-tuple-element.36) | copy-start | bytes 12292
  142.6 4.8 %copy-start.8 = (f32[1024]{0:T(1024)S(1)}, f32[1024]{0:T(1024)}, u32[]{:S(2)}) copy-start(f32[1024]{0:T(1024)} %get-tuple-element.37) | copy-start | bytes 12292
  143.7 5.1 %copy-start.5 = (f32[1024]{0:T(1024)S(1)}, f32[1024]{0:T(1024)}, u32[]{:S(2)}) copy-start(f32[1024]{0:T(1024)} %get-tuple-element.34) | copy-start | bytes 12292
  143.7 5.1 %copy-start.6 = (f32[1024]{0:T(1024)S(1)}, f32[1024]{0:T(1024)}, u32[]{:S(2)}) copy-start(f32[1024]{0:T(1024)} %get-tuple-element.35) | copy-start | bytes 12292
  147.4 7.7 %copy-start.3 = (f32[1024]{0:T(1024)S(1)}, f32[1024]{0:T(1024)}, u32[]{:S(2)}) copy-start(f32[1024]{0:T(1024)} %get-tuple-element.32) | copy-start | bytes 12292
  147.4 7.7 %copy-start.4 = (f32[1024]{0:T(1024)S(1)}, f32[1024]{0:T(1024)}, u32[]{:S(2)}) copy-start(f32[1024]{0:T(1024)} %get-tuple-element.33) | copy-start | bytes 12292
  147.4 7.7 %collective-permute-start.16 = (bf16[128,1024]{0,1:T(8,128)(2,1)}, bf16[128,1024]{0,1:T(8,128)(2,1)S(1)}, u32[]{:S(2)}, u32[]{:S(2)}) collective-permute-start(bf16[128,1024]{0,1:T(8,128)(2,1)} %collective-permute-done.14), channel_id=1, source_target_pairs={{4,8},{8,12},{12,14},{14,10},{10,6},{6,2},{2,0},{0,4},{5,9},{9,13}... | collective-permute-start | bytes 786440 | tf_op jit(solution)/shard_map/ppermute | solution.py:163
  150.4 6.6 %collective-permute-start.17 = (bf16[128,1024]{0,1:T(8,128)(2,1)}, bf16[128,1024]{0,1:T(8,128)(2,1)S(1)}, u32[]{:S(2)}, u32[]{:S(2)}) collective-permute-start(bf16[128,1024]{0,1:T(8,128)(2,1)} %collective-permute-done.15), channel_id=1, source_target_pairs={{8,4},{12,8},{14,12},{10,14},{6,10},{2,6},{0,2},{4,0},{9,5},{13,9}... | collective-permute-start | bytes 786440 | tf_op jit(solution)/shard_map/ppermute | solution.py:166
  155.1 8.1 %collective-permute-start.18 = (bf16[128,1024]{0,1:T(8,128)(2,1)S(1)}, bf16[128,1024]{0,1:T(8,128)(2,1)S(1)}, u32[]{:S(2)}, u32[]{:S(2)}) collective-permute-start(bf16[128,1024]{0,1:T(8,128)(2,1)S(1)} %collective-permute-done.16), channel_id=1, source_target_pairs={{4,8},{8,12},{12,14},{14,10},{10,6},{6,2},{2,0},{0,4},{5,9},{9,13}... | collective-permute-start | bytes 786440 | tf_op jit(solution)/shard_map/ppermute | solution.py:163
  157.1 0.7 copy-start.12
  158.4 6.6 %collective-permute-start.19 = (bf16[128,1024]{0,1:T(8,128)(2,1)}, bf16[128,1024]{0,1:T(8,128)(2,1)S(1)}, u32[]{:S(2)}, u32[]{:S(2)}) collective-permute-start(bf16[128,1024]{0,1:T(8,128)(2,1)} %copy-done.12), channel_id=1, source_target_pairs={{8,4},{12,8},{14,12},{10,14},{6,10},{2,6},{0,2},{4,0},{9,5},{13,9}... | collective-permute-start | bytes 786440 | tf_op jit(solution)/shard_map/ppermute | solution.py:166
  163.2 6.4 %collective-permute-start.20 = (bf16[128,1024]{0,1:T(8,128)(2,1)S(1)}, bf16[128,1024]{0,1:T(8,128)(2,1)S(1)}, u32[]{:S(2)}, u32[]{:S(2)}) collective-permute-start(bf16[128,1024]{0,1:T(8,128)(2,1)S(1)} %collective-permute-done.18), channel_id=1, source_target_pairs={{4,8},{8,12},{12,14},{14,10},{10,6},{6,2},{2,0},{0,4},{5,9},{9,13}... | collective-permute-start | bytes 786440 | tf_op jit(solution)/shard_map/ppermute | solution.py:163
